TPU v7x, 32 devices: a whole 2x2x4 slice. The times are simulated.
32 devices in a mesh: owner: 2 (over x), reader: 16 (over z, y, core).
Axes of the slice: x: 2, y: 2, z: 4, core: 2. Of those that a mesh axis runs over, the one named last changes fastest.
Arguments:
- acts: bfloat16 [256, 4096], P('reader', 'owner'), may hold values from -6 to 6
- grads: bfloat16 [256, 14336], P('reader', 'owner'), may hold values from -6 to 6
- basis_a: bfloat16 [4096, 4096], P('reader', 'owner'), may hold values from -0.09375 to 0.09375
- basis_g: bfloat16 [14336, 14336], P('reader', 'owner'), may hold values from -0.046875 to 0.046875
- eigvals: bfloat16 [14336, 4096], P('reader', 'owner'), may hold values from 0.099609375 to 10
- lengths: int32 [2], replicated, may hold values from 1 to 128, as said below
- shuffle: int32 [2], replicated, may hold values from 0 to 1, each once
Outputs:
- token_score: float32 [256], P('owner')
- example_score: float32 [2], replicated
Inputs may be any that keep to these rules, and one draw needn't show every extreme that they name: `lengths`: some slot has exactly 128 live tokens. `shuffle`: each example id appears once.
All inputs are finite; a program needn't handle non-finite values.
Results may differ from a plain program's by a relative error of at most 0.0003.
Values may be sent and summed in bfloat16 or wider, within the bound.
No kernel may reach another device: no remote copies, remote signals or barrier semaphores. Data moves between devices by JAX's collectives and lax.ppermute only.
A program may use at most 128 MiB of HBM per device.

v0:
```python
import jax
import jax.numpy as jnp
from jax import lax
from jax.sharding import PartitionSpec as P

D = 4096
FF = 14336
SEQ = 128


def local(acts, grads, basis_a, basis_g, eigvals, lengths, shuffle):
    owner_index = lax.axis_index("owner")
    own_length = lax.dynamic_index_in_dim(lengths, owner_index, 0, keepdims=False)
    positions = jnp.arange(SEQ, dtype=jnp.int32)
    live = (positions < own_length).astype(jnp.float32)
    partial_g = jnp.einsum(
        "tk,jk->tj",
        lax.all_gather(grads, "reader", axis=0, tiled=True),
        basis_g,
        preferred_element_type=jnp.float32,
    )
    own_g = lax.psum_scatter(partial_g, "owner", scatter_dimension=0, tiled=True)
    rot_g = (own_g * live[:, None]).astype(jnp.bfloat16)
    all_rows = lax.all_gather(acts, "reader", axis=0, tiled=True)
    own_rows = lax.all_to_all(all_rows, "owner", split_axis=0, concat_axis=1, tiled=True)
    vectors = lax.all_gather(basis_a, "owner", axis=1, tiled=True)
    own_a = jnp.einsum("tk,jk->tj", own_rows, vectors, preferred_element_type=jnp.float32)
    rot_a = (own_a * live[:, None]).astype(jnp.bfloat16)
    full_a = lax.all_gather(rot_a, "reader", axis=1, tiled=True)
    eigen_block = lax.all_gather(eigvals, "owner", axis=1, tiled=True)
    outer = jnp.einsum("tm,tn->mn", rot_g, full_a, preferred_element_type=jnp.float32)
    scaled = (outer / eigen_block.astype(jnp.float32)).astype(jnp.bfloat16)
    projected = jnp.dot(rot_g, scaled, preferred_element_type=jnp.float32)
    partial_score = jnp.sum(projected * full_a.astype(jnp.float32), axis=1) / (FF * D)
    token_score = lax.psum(partial_score, "reader")
    slot_mean = jnp.sum(token_score, keepdims=True) / SEQ
    all_means = lax.all_gather(slot_mean, "owner", axis=0, tiled=True)
    count = shuffle.shape[0]
    table = (shuffle[:, None] == jnp.arange(count, dtype=jnp.int32)[None, :]).astype(jnp.float32)
    example_score = jnp.sum(all_means[:, None] * table, axis=0)
    return (token_score, example_score)


def solution(mesh):
    return jax.shard_map(
        local,
        mesh=mesh,
        in_specs=(
            P("reader", "owner"),
            P("reader", "owner"),
            P("reader", "owner"),
            P("reader", "owner"),
            P("reader", "owner"),
            P(),
            P(),
        ),
        out_specs=(P("owner"), P()),
        check_vma=False,
    )
```

profile of v0, /device:TPU:0, one launch (start us, length us, event | category | flops | bytes accessed | tf_op | source)
XLA Modules:
  0.0 346.0 jit_solution(8944493307228276584)
XLA Ops:
  7.2 0.7 all-gather.8.cloned.1.call-update
  7.9 0.7 all-gather.10.cloned.1.call-update
  8.7 0.7 all-gather.6.cloned.1.call-update
  9.4 41.5 %all-gather.8.cloned.1.call-done = bf16[256,2048]{1,0:T(8,128)(2,1)} async-done(((bf16[16,2048]{1,0:T(8,128)(2,1)}), bf16[256,2048]{1,0:T(8,128)(2,1)}) %all-gather.8.cloned.1.call-update) | async-done | bytes 1048592 | tf_op jit(solution)/shard_map/all_gather | solution.py:24
  50.8 3.6 %all-to-all-start = ((bf16[2,128,2048]{2,1,0:T(8,128)(2,1)}), bf16[2,128,2048]{2,1,0:T(8,128)(2,1)S(1)}, u32[]{:S(2)}, u32[]{:S(2)}) async-start(bf16[2,128,2048]{2,1,0:T(8,128)(2,1)} %bitcast.13), calls=%async_computation.1 | async-start | bytes 2097152 | tf_op jit(solution)/shard_map/all_to_all | solution.py:25
  54.5 1.2 dynamic_slice.4
  55.7 0.6 compare_convert_fusion
  56.4 19.8 %all-to-all-done = bf16[2,128,2048]{2,1,0:T(8,128)(2,1)S(1)} async-done(((bf16[2,128,2048]{2,1,0:T(8,128)(2,1)}), bf16[2,128,2048]{2,1,0:T(8,128)(2,1)S(1)}, u32[]{:S(2)}, u32[]{:S(2)}) %all-to-all-start) | async-done | bytes 1048608 | tf_op jit(solution)/shard_map/all_to_all | solution.py:25
  76.2 0.7 copy.10
  76.9 14.5 %all-gather.10.cloned.1.call-done = bf16[256,4096]{1,0:T(8,128)(2,1)} async-done(((bf16[256,2048]{1,0:T(8,128)(2,1)}), bf16[256,4096]{1,0:T(8,128)(2,1)}) %all-gather.10.cloned.1.call-update) | async-done | bytes 2097168 | tf_op jit(solution)/shard_map/all_gather | solution.py:26
  91.4 3.1 fusion.5
  94.6 0.5 all-gather.14.cloned.1.call-update
  95.2 44.1 %all-gather.6.cloned.1.call-done = bf16[256,7168]{1,0:T(8,128)(2,1)} async-done(((bf16[16,7168]{1,0:T(8,128)(2,1)}), bf16[256,7168]{1,0:T(8,128)(2,1)}) %all-gather.6.cloned.1.call-update) | async-done | bytes 3670032 | tf_op jit(solution)/shard_map/all_gather | solution.py:18
  139.3 10.7 %fusion.9 = f32[256,896]{1,0:T(8,128)} fusion(bf16[256,7168]{1,0:T(8,128)(2,1)} %all-gather.6.cloned.1.call-done, bf16[896,7168]{1,0:T(8,128)(2,1)} %param.10), kind=kOutput, calls=%fused_computation.13 | convolution fusion | flops 3288334336 | bytes 17432576 | tf_op jit(solution)/shard_map/tk,jk->tj/dot_general | solution.py:16
  150.0 0.6 dynamic-slice
  150.5 26.6 %all-gather.12.cloned.1.call-done = bf16[128,4096]{1,0:T(8,128)(2,1)} async-done(((bf16[128,256]{1,0:T(8,128)(2,1)}), bf16[128,4096]{1,0:T(8,128)(2,1)}) %all-gather.12.cloned.1.call-update) | async-done | bytes 1048592 | tf_op jit(solution)/shard_map/all_gather | solution.py:29
  177.1 93.1 %all-gather.14.cloned.1.call-done = bf16[896,4096]{1,0:T(8,128)(2,1)} async-done(((bf16[896,2048]{1,0:T(8,128)(2,1)}), bf16[896,4096]{1,0:T(8,128)(2,1)}) %all-gather.14.cloned.1.call-update) | async-done | bytes 7340048 | tf_op jit(solution)/shard_map/all_gather | solution.py:30
  270.3 21.0 %reduce-scatter.2.cloned.1.call-done = f32[128,896]{1,0:T(8,128)} async-done(((f32[256,896]{1,0:T(8,128)}), f32[128,896]{1,0:T(8,128)}) %reduce-scatter.2.cloned.1.call-update) | async-done | bytes 458768 | tf_op jit(solution)/shard_map/reduce_scatter | solution.py:22
  291.3 7.3 %fusion.4 = f32[128]{0:T(128)S(1)} fusion(bf16[128,4096]{1,0:T(8,128)(2,1)} %all-gather.12.cloned.1.call-done, bf16[896,4096]{1,0:T(8,128)(2,1)} %all-gather.14.cloned.1.call-done, f32[128,896]{1,0:T(8,128)} %reduce-scatter.2.cloned.1.call-done, f32[128]{0:T(128)S(1)} %compare_convert_fusion), kind=kOutput, calls=%fused_computation.4 | convolution fusion | flops 1892089728 | bytes 8848384 | tf_op jit(solution)/shard_map/dot_general | solution.py:33
  298.6 33.2 %psum.7 = f32[128]{0:T(128)S(1)} all-reduce(f32[128]{0:T(128)S(1)} %broadcast_multiply_fusion), channel_id=1, replica_groups=mesh['owner'=2,'reader'=16] {'reader'}, use_global_device_ids=true, to_apply=%region_2.3 | all-reduce | flops 128 | bytes 1024 | tf_op jit(solution)/shard_map/psum | solution.py:35
  331.7 0.6 reduce_sum.28
  333.0 0.7 dynamic-update-slice
  333.7 4.9 %all-reduce = f32[2]{0:T(128)S(1)} all-reduce(f32[2]{0:T(128)S(1)} %dynamic-update-slice), channel_id=1, replica_groups=mesh['owner'=2,'reader'=16] {'owner'}, use_global_device_ids=true, to_apply=%add | all-reduce | flops 2 | bytes 16
  338.6 0.6 fusion.8
  (16 shorter events, 0.3 us)
Async XLA Ops:
  7.2 43.7 %all-gather.8.cloned.1.call-start = ((), (), s32[]{:S(2)}) async-start(), calls=%async_computation.4 | async-start | bytes 1114112 | tf_op jit(solution)/shard_map/all_gather | solution.py:24
  7.9 83.5 %all-gather.10.cloned.1.call-start = ((), (), s32[]{:S(2)}) async-start(), calls=%async_computation.5 | async-start | bytes 3145728 | tf_op jit(solution)/shard_map/all_gather | solution.py:26
  8.6 130.6 %all-gather.6.cloned.1.call-start = ((), (), s32[]{:S(2)}) async-start(), calls=%async_computation.2 | async-start | bytes 3899392 | tf_op jit(solution)/shard_map/all_gather | solution.py:18
  50.8 25.4 %all-to-all-start = ((bf16[2,128,2048]{2,1,0:T(8,128)(2,1)}), bf16[2,128,2048]{2,1,0:T(8,128)(2,1)S(1)}, u32[]{:S(2)}, u32[]{:S(2)}) async-start(bf16[2,128,2048]{2,1,0:T(8,128)(2,1)} %bitcast.13), calls=%async_computation.1 | async-start | bytes 2097152 | tf_op jit(solution)/shard_map/all_to_all | solution.py:25
  54.4 122.7 %all-gather.12.cloned.1.call-start = ((), (), s32[]{:S(2)}) async-start(), calls=%async_computation.6 | async-start | bytes 1114112 | tf_op jit(solution)/shard_map/all_gather | solution.py:29
  94.5 175.7 %all-gather.14.cloned.1.call-start = ((), (), s32[]{:S(2)}) async-start(), calls=%async_computation.7 | async-start | bytes 11010048 | tf_op jit(solution)/shard_map/all_gather | solution.py:30
  95.1 54.9 %copy-start.1 = (u32[32]{0:T(128)S(1)}, u32[32]{0:T(128)}, u32[]{:S(2)}) copy-start(u32[32]{0:T(128)} %constant.24) | copy-start | bytes 388
  95.1 196.1 %reduce-scatter.2.cloned.1.call-start = ((), (), s32[]{:S(2)}) async-start(), calls=%async_computation.3 | async-start | bytes 1376256 | tf_op jit(solution)/shard_map/reduce_scatter | solution.py:22
  150.5 188.0 %copy-start = (s32[2]{0:T(128)S(1)}, s32[2]{0:T(128)}, u32[]{:S(2)}) copy-start(s32[2]{0:T(128)} %param.13) | copy-start | bytes 28
  331.7 7.4 %copy-start.2 = (f32[128]{0:T(128)}, f32[128]{0:T(128)S(1)}, u32[]{:S(2)}) copy-start(f32[128]{0:T(128)S(1)} %psum.7) | copy-start | bytes 1540
Sparse Core Ops, SparseCore 0:
  10.2 40.6 all-gather.7
  52.4 39.0 all-gather.9
  93.7 45.4 all-gather.5
  141.3 35.8 all-gather.11
  178.5 91.6 all-gather.13
  272.4 18.8 reduce-scatter.1
where the time goes:
time: 346 us
  waiting for transfers between devices  263 us (76%)
  blocking collectives  38.1 us (11%)
  matrix products  21.1 us (6%)
  between operations  14.8 us (4%)
  starting transfers between devices  3.81 us (1%)
    all_gather x1, waiting for transfers between devices, local(): eigen_block = lax.all_gather(eigvals, 'owner', axis=1, tiled=True)  93.1 us
    all_gather x1, waiting for transfers between devices, local(): lax.all_gather(grads, 'reader', axis=0, tiled=True)  44.1 us
    all_gather x1, waiting for transfers between devices, local(): all_rows = lax.all_gather(acts, 'reader', axis=0, tiled=True)  41.5 us
    psum x1, blocking collectives, local(): token_score = lax.psum(partial_score, 'reader')  33.2 us
    all_gather x1, waiting for transfers between devices, local(): full_a = lax.all_gather(rot_a, 'reader', axis=1, tiled=True)  26.6 us
    reduce_scatter x1, waiting for transfers between devices, local(): lax.psum_scatter(partial_g, 'owner', scatter_dimension=0, tiled=True)  21 us
    all_to_all x1, waiting for transfers between devices, local(): lax.all_to_all(all_rows, 'owner', split_axis=0, concat_axis=1, tiled=True)  19.8 us
    all_gather x1, waiting for transfers between devices, local(): vectors = lax.all_gather(basis_a, 'owner', axis=1, tiled=True)  14.5 us
  transfers between devices with their start and end apart: 7, of which 7 were waited for; matrix products, arithmetic and copies ran while one was open for 5% of the time, Pallas kernels for 0%

commit v1 on v0

--- a/solution.py
+++ b/solution.py
@@ -22,7 +22,12 @@
     own_g = lax.psum_scatter(partial_g, "owner", scatter_dimension=0, tiled=True)
     rot_g = (own_g * live[:, None]).astype(jnp.bfloat16)
     all_rows = lax.all_gather(acts, "reader", axis=0, tiled=True)
-    own_rows = lax.all_to_all(all_rows, "owner", split_axis=0, concat_axis=1, tiled=True)
+    own_rows = jnp.concatenate(
+        lax.all_to_all(
+            jnp.stack(jnp.split(all_rows, lax.axis_size("owner"), axis=0)), "owner", 0, 0
+        ),
+        axis=1,
+    )
     vectors = lax.all_gather(basis_a, "owner", axis=1, tiled=True)
     own_a = jnp.einsum("tk,jk->tj", own_rows, vectors, preferred_element_type=jnp.float32)
     rot_a = (own_a * live[:, None]).astype(jnp.bfloat16)

time: 346 us -> 349 us (level)
    all_gather x1, waiting for transfers between devices: 14.5 us -> 35.7 us  [local(): vectors = lax.all_gather(basis_a, 'owner', axis=1, tiled=True)]
    all_to_all x1, waiting for transfers between devices: 19.8 us -> 0.01 us  [local(): lax.all_to_all(jnp.stack(jnp.split(all_rows, lax.axis_size('owner'), axis...]
  transfers between devices with their start and end apart: 7 -> 7, of which waited for: 7 -> 6; matrix products, arithmetic and copies ran while one was open for 5% -> 5% of each run, Pallas kernels for 0% -> 0%
where the time goes in v1:
time: 349 us
  waiting for transfers between devices  264 us (76%)
  blocking collectives  38.1 us (11%)
  matrix products  21 us (6%)
  between operations  14.9 us (4%)
  local copies, waits for them, and re-layouts  3.86 us (1%)
  starting transfers between devices  3.81 us (1%)
    all_gather x1, waiting for transfers between devices, local(): eigen_block = lax.all_gather(eigvals, 'owner', axis=1, tiled=True)  93.1 us
    all_gather x1, waiting for transfers between devices, local(): lax.all_gather(grads, 'reader', axis=0, tiled=True)  44.1 us
    all_gather x1, waiting for transfers between devices, local(): all_rows = lax.all_gather(acts, 'reader', axis=0, tiled=True)  41.5 us
    all_gather x1, waiting for transfers between devices, local(): vectors = lax.all_gather(basis_a, 'owner', axis=1, tiled=True)  35.7 us
    psum x1, blocking collectives, local(): token_score = lax.psum(partial_score, 'reader')  33.2 us
    all_gather x1, waiting for transfers between devices, local(): full_a = lax.all_gather(rot_a, 'reader', axis=1, tiled=True)  26.5 us
    reduce_scatter x1, waiting for transfers between devices, local(): lax.psum_scatter(partial_g, 'owner', scatter_dimension=0, tiled=True)  21 us
    dot_general x1, matrix products, local(): jnp.einsum('tk,jk->tj', lax.all_gather(grads, 'reader', axis=0, tiled=Tru...  10.7 us
  transfers between devices with their start and end apart: 7, of which 6 were waited for; matrix products, arithmetic and copies ran while one was open for 5% of the time, Pallas kernels for 0%

profile of v1, /device:TPU:0, one launch (start us, length us, event | category | flops | bytes accessed | tf_op | source)
XLA Modules:
  0.0 349.1 jit_solution(17200239072719104446)
XLA Ops:
  7.2 0.7 all-gather.8.cloned.1.call-update
  8.0 0.7 all-gather.10.cloned.1.call-update
  8.7 0.7 all-gather.6.cloned.1.call-update
  9.4 41.5 %all-gather.8.cloned.1.call-done = bf16[256,2048]{1,0:T(8,128)(2,1)} async-done(((bf16[16,2048]{1,0:T(8,128)(2,1)}), bf16[256,2048]{1,0:T(8,128)(2,1)}) %all-gather.8.cloned.1.call-update) | async-done | bytes 1048592 | tf_op jit(solution)/shard_map/all_gather | solution.py:24
  50.8 1.3 fusion.9
  52.7 1.1 pad_maximum_fusion
  53.8 3.6 %all-to-all-start = ((bf16[2,128,2048]{1,2,0:T(8,128)(2,1)}), bf16[2,128,2048]{1,2,0:T(8,128)(2,1)S(1)}, u32[]{:S(2)}, u32[]{:S(2)}) async-start(bf16[2,128,2048]{1,2,0:T(8,128)(2,1)} %pad_maximum_fusion), calls=%async_computation.1 | async-start | bytes 2097152 | tf_op jit(solution)/shard_map/all_to_all | solution.py:26
  57.4 0.6 dynamic_slice.4
  58.0 0.7 compare_convert_fusion
  58.7 35.7 %all-gather.10.cloned.1.call-done = bf16[256,4096]{1,0:T(8,128)(2,1)} async-done(((bf16[256,2048]{1,0:T(8,128)(2,1)}), bf16[256,4096]{1,0:T(8,128)(2,1)}) %all-gather.10.cloned.1.call-update) | async-done | bytes 2097168 | tf_op jit(solution)/shard_map/all_gather | solution.py:31
  94.3 3.1 fusion.5
  97.5 0.5 all-gather.14.cloned.1.call-update
  98.1 44.1 %all-gather.6.cloned.1.call-done = bf16[256,7168]{1,0:T(8,128)(2,1)} async-done(((bf16[16,7168]{1,0:T(8,128)(2,1)}), bf16[256,7168]{1,0:T(8,128)(2,1)}) %all-gather.6.cloned.1.call-update) | async-done | bytes 3670032 | tf_op jit(solution)/shard_map/all_gather | solution.py:18
  142.2 10.7 %fusion.10 = f32[256,896]{1,0:T(8,128)} fusion(bf16[256,7168]{1,0:T(8,128)(2,1)} %all-gather.6.cloned.1.call-done, bf16[896,7168]{1,0:T(8,128)(2,1)} %param.10), kind=kOutput, calls=%fused_computation.15 | convolution fusion | flops 3288334336 | bytes 17432576 | tf_op jit(solution)/shard_map/tk,jk->tj/dot_general | solution.py:16
  152.9 0.7 dynamic-slice
  153.6 26.5 %all-gather.12.cloned.1.call-done = bf16[128,4096]{1,0:T(8,128)(2,1)} async-done(((bf16[128,256]{1,0:T(8,128)(2,1)}), bf16[128,4096]{1,0:T(8,128)(2,1)}) %all-gather.12.cloned.1.call-update) | async-done | bytes 1048592 | tf_op jit(solution)/shard_map/all_gather | solution.py:34
  180.1 93.1 %all-gather.14.cloned.1.call-done = bf16[896,4096]{1,0:T(8,128)(2,1)} async-done(((bf16[896,2048]{1,0:T(8,128)(2,1)}), bf16[896,4096]{1,0:T(8,128)(2,1)}) %all-gather.14.cloned.1.call-update) | async-done | bytes 7340048 | tf_op jit(solution)/shard_map/all_gather | solution.py:35
  273.2 21.0 %reduce-scatter.2.cloned.1.call-done = f32[128,896]{1,0:T(8,128)} async-done(((f32[256,896]{1,0:T(8,128)}), f32[128,896]{1,0:T(8,128)}) %reduce-scatter.2.cloned.1.call-update) | async-done | bytes 458768 | tf_op jit(solution)/shard_map/reduce_scatter | solution.py:22
  294.2 7.3 %fusion.4 = f32[128]{0:T(128)S(1)} fusion(bf16[128,4096]{1,0:T(8,128)(2,1)} %all-gather.12.cloned.1.call-done, bf16[896,4096]{1,0:T(8,128)(2,1)} %all-gather.14.cloned.1.call-done, f32[128,896]{1,0:T(8,128)} %reduce-scatter.2.cloned.1.call-done, f32[128]{0:T(128)S(1)} %compare_convert_fusion), kind=kOutput, calls=%fused_computation.4 | convolution fusion | flops 1892089728 | bytes 8848384 | tf_op jit(solution)/shard_map/dot_general | solution.py:38
  301.5 33.2 %psum.7 = f32[128]{0:T(128)S(1)} all-reduce(f32[128]{0:T(128)S(1)} %broadcast_multiply_fusion), channel_id=1, replica_groups=mesh['owner'=2,'reader'=16] {'reader'}, use_global_device_ids=true, to_apply=%region_2.3 | all-reduce | flops 128 | bytes 1024 | tf_op jit(solution)/shard_map/psum | solution.py:40
  334.6 0.6 reduce_sum.28
  335.9 0.8 dynamic-update-slice
  336.7 4.9 %all-reduce = f32[2]{0:T(128)S(1)} all-reduce(f32[2]{0:T(128)S(1)} %dynamic-update-slice), channel_id=1, replica_groups=mesh['owner'=2,'reader'=16] {'owner'}, use_global_device_ids=true, to_apply=%add | all-reduce | flops 2 | bytes 16
  341.6 0.6 fusion.8
  (21 shorter events, 0.8 us)
Async XLA Ops:
  7.2 50.2 %copy-start = (s32[2]{0:T(128)S(1)}, s32[2]{0:T(128)}, u32[]{:S(2)}) copy-start(s32[2]{0:T(128)} %param.12) | copy-start | bytes 28
  7.2 43.7 %all-gather.8.cloned.1.call-start = ((), (), s32[]{:S(2)}) async-start(), calls=%async_computation.4 | async-start | bytes 1114112 | tf_op jit(solution)/shard_map/all_gather | solution.py:24
  7.9 86.4 %all-gather.10.cloned.1.call-start = ((), (), s32[]{:S(2)}) async-start(), calls=%async_computation.5 | async-start | bytes 3145728 | tf_op jit(solution)/shard_map/all_gather | solution.py:31
  8.7 133.5 %all-gather.6.cloned.1.call-start = ((), (), s32[]{:S(2)}) async-start(), calls=%async_computation.2 | async-start | bytes 3899392 | tf_op jit(solution)/shard_map/all_gather | solution.py:18
  53.8 40.6 %all-to-all-start = ((bf16[2,128,2048]{1,2,0:T(8,128)(2,1)}), bf16[2,128,2048]{1,2,0:T(8,128)(2,1)S(1)}, u32[]{:S(2)}, u32[]{:S(2)}) async-start(bf16[2,128,2048]{1,2,0:T(8,128)(2,1)} %pad_maximum_fusion), calls=%async_computation.1 | async-start | bytes 2097152 | tf_op jit(solution)/shard_map/all_to_all | solution.py:26
  57.3 122.7 %all-gather.12.cloned.1.call-start = ((), (), s32[]{:S(2)}) async-start(), calls=%async_computation.6 | async-start | bytes 1114112 | tf_op jit(solution)/shard_map/all_gather | solution.py:34
  97.4 175.7 %all-gather.14.cloned.1.call-start = ((), (), s32[]{:S(2)}) async-start(), calls=%async_computation.7 | async-start | bytes 11010048 | tf_op jit(solution)/shard_map/all_gather | solution.py:35
  98.0 54.9 %copy-start.2 = (u32[32]{0:T(128)S(1)}, u32[32]{0:T(128)}, u32[]{:S(2)}) copy-start(u32[32]{0:T(128)} %constant.24) | copy-start | bytes 388
  98.0 196.1 %reduce-scatter.2.cloned.1.call-start = ((), (), s32[]{:S(2)}) async-start(), calls=%async_computation.3 | async-start | bytes 1376256 | tf_op jit(solution)/shard_map/reduce_scatter | solution.py:22
  153.6 188.1 %copy-start.1 = (s32[2]{0:T(128)S(1)}, s32[2]{0:T(128)}, u32[]{:S(2)}) copy-start(s32[2]{0:T(128)} %param.13) | copy-start | bytes 28
  334.6 7.6 %copy-start.3 = (f32[128]{0:T(128)}, f32[128]{0:T(128)S(1)}, u32[]{:S(2)}) copy-start(f32[128]{0:T(128)S(1)} %psum.7) | copy-start | bytes 1540
Sparse Core Ops, SparseCore 0:
  10.2 40.6 all-gather.7
  52.4 41.9 all-gather.9
  96.6 45.4 all-gather.5
  144.2 35.8 all-gather.11
  181.5 91.6 all-gather.13
  275.3 18.8 reduce-scatter.1
